TPU v7x, 32 devices: a whole 2x2x4 slice. The times are simulated.
32 devices in a mesh: groups: 2 (over y), replica: 4 (over z), tensor: 4 (over x, core).
Axes of the slice: x: 2, y: 2, z: 4, core: 2. Of those that a mesh axis runs over, the one named last changes fastest.
Arguments:
- queries: bfloat16 [8, 128, 8192], P(('groups', 'replica'), None, 'tensor'), parts along dimension 0, may hold values from -12 to 12
- suffix_kv: bfloat16 [8, 2, 128, 1024], P(('groups', 'replica'), None, None, 'tensor'), parts along dimension 0, may hold values from -12 to 12
- page_pool: bfloat16 [96, 2, 128, 1024], P(('groups', 'replica'), None, 'tensor'), parts along dimension 0, may hold values from -6 to 6
- offsets: int32 [8, 8], P('groups'), parts along dimension 0, may hold values from 1 to 3, as said below
- slots: int32 [8, 8], P('groups'), parts along dimension 0, may hold values from 0 to 11, as said below
- prefix_len: int32 [8], P('groups'), parts along dimension 0, may hold values from 1 to 1024, 2048 in all
Outputs:
- attended: bfloat16 [8, 128, 8192], P(('groups', 'replica'), None, 'tensor'), parts along dimension 0
There are 2 independent parts, one for each index of `groups`. A program takes and returns all parts, laid end to end along the dimension named above; each array names one. Nothing has to cross between parts.
Inputs may be any that keep to these rules, and one draw needn't show every extreme that they name: Page p of request r is held by replica (r - offsets[r, p]) mod 4; one request takes at most 4 pages from one holder, and exactly 4 from some holder. `slots`: the prefix pages of one request are distinct pool entries. `prefix_len`: the longest prefix fills all 8 pages.
All inputs are finite; a program needn't handle non-finite values.
Results may differ from a plain program's by a relative error of at most 0.0034.
Values may be sent and summed in bfloat16 or wider, within the bound.
No kernel may reach another device: no remote copies, remote signals or barrier semaphores. Data moves between devices by JAX's collectives and lax.ppermute only.
A program may use at most 64 MiB of HBM per device.

v0:
```python
import math
import jax
import jax.numpy as jnp
from jax import lax
from jax.sharding import PartitionSpec as P

HEADS = 64
KV_HEADS = 8
HEAD_DIM = 128
NEG_FILL = -1e30


def passed_along(value, axis, steps):
    count = lax.axis_size(axis)
    pairs = [(source, (source + steps) % count) for source in range(count)]
    return lax.ppermute(value, axis, pairs)


def absorb(state_now, scores, visible, values):
    run_max, run_sum, run_acc = state_now
    masked = jnp.where(visible, scores, NEG_FILL)
    new_max = jnp.maximum(run_max, jnp.max(masked, axis=-1))
    weights = jnp.where(visible, jnp.exp(masked - new_max[..., None]), 0.0)
    rescale = jnp.exp(run_max - new_max)
    run_sum = run_sum * rescale + jnp.sum(weights, axis=-1)
    update = jnp.einsum(
        "kgqc,ckd->kgqd", weights.astype(jnp.bfloat16), values, preferred_element_type=jnp.float32
    )
    run_acc = run_acc * rescale[..., None] + update
    return (new_max, run_sum, run_acc)


def pack_pages(pool_part, offsets, slots, holder, replicas, span_count, slot_cap):
    distances = jnp.arange(1, span_count + 1, dtype=jnp.int32)
    readers = (holder + distances) % replicas
    off_rows = jnp.take(offsets, readers, axis=0)
    slot_rows = jnp.take(slots, readers, axis=0)
    matched = (off_rows == distances[:, None]).astype(jnp.int32)
    ranking = jnp.cumsum(matched, axis=1) - 1
    places = jnp.arange(slot_cap, dtype=jnp.int32)
    picked = matched[:, None, :] * (ranking[:, None, :] == places[None, :, None]).astype(jnp.int32)
    chosen = jnp.sum(picked * slot_rows[:, None, :], axis=2)
    gathered = jnp.take(pool_part, chosen.reshape(-1), axis=0)
    return gathered.reshape((span_count, slot_cap) + pool_part.shape[1:])


def page_index(own_offsets, slot_cap):
    page_count = own_offsets.shape[0]
    same_holder = own_offsets[:, None] == own_offsets[None, :]
    counter = jnp.arange(page_count, dtype=jnp.int32)
    earlier = counter[None, :] < counter[:, None]
    ranking = jnp.sum((same_holder & earlier).astype(jnp.int32), axis=1)
    return (own_offsets - 1) * slot_cap + ranking


def on_device(queries, suffix_kv, page_pool, offsets, slots, prefix_len):
    replicas = lax.axis_size("replica")
    reader = lax.axis_index("replica")
    span_count = min(8, replicas - 1)
    page_count = offsets.shape[1]
    slot_cap = (page_count + span_count - 1) // span_count + 1
    own_offsets = lax.dynamic_index_in_dim(offsets, reader, 0, keepdims=False)
    own_length = lax.dynamic_index_in_dim(prefix_len, reader, 0, keepdims=False)
    source = lax.all_to_all(page_pool, "tensor", split_axis=3, concat_axis=2, tiled=True)
    payload = pack_pages(source, offsets, slots, reader, replicas, span_count, slot_cap)
    arrivals = []
    for distance in range(1, span_count + 1):
        arrivals.append(passed_along(payload[distance - 1], "replica", distance))
    arrived = jnp.stack(arrivals)
    flattened = arrived.reshape((span_count * slot_cap,) + arrived.shape[2:])
    fetched = jnp.take(flattened, page_index(own_offsets, slot_cap), axis=0)
    width = fetched.shape[3]
    kv_local = width // HEAD_DIM
    group = HEADS // KV_HEADS
    suffix_rows = queries.shape[1]
    prefix_rows = page_count * fetched.shape[2]
    scale = HEAD_DIM ** (-0.5)
    query_heads = queries[0].reshape(suffix_rows, kv_local, group, HEAD_DIM)
    suffix_keys = suffix_kv[0, 0].reshape(suffix_rows, kv_local, HEAD_DIM)
    suffix_vals = suffix_kv[0, 1].reshape(suffix_rows, kv_local, HEAD_DIM)
    initial = (
        jnp.full((kv_local, group, suffix_rows), NEG_FILL, jnp.float32),
        jnp.zeros((kv_local, group, suffix_rows), jnp.float32),
        jnp.zeros((kv_local, group, suffix_rows, HEAD_DIM), jnp.float32),
    )
    suffix_scores = (
        jnp.einsum("qkgd,ckd->kgqc", query_heads, suffix_keys, preferred_element_type=jnp.float32)
        * scale
    )
    query_pos = jnp.arange(suffix_rows, dtype=jnp.int32)
    causal = query_pos[:, None] >= query_pos[None, :]
    state_now = absorb(initial, suffix_scores, causal, suffix_vals)
    block_rows = math.gcd(prefix_rows, 512)
    block_count = prefix_rows // block_rows
    prefix_keys = fetched[:, 0].reshape(block_count, block_rows, kv_local, HEAD_DIM)
    prefix_vals = fetched[:, 1].reshape(block_count, block_rows, kv_local, HEAD_DIM)
    block_pos = jnp.arange(block_rows, dtype=jnp.int32)

    def visit(state_in, pieces):
        keys_block, vals_block, first_row = pieces
        block_scores = (
            jnp.einsum(
                "qkgd,ckd->kgqc", query_heads, keys_block, preferred_element_type=jnp.float32
            )
            * scale
        )
        visible = first_row + block_pos < own_length
        return (absorb(state_in, block_scores, visible, vals_block), None)

    starts = jnp.arange(block_count, dtype=jnp.int32) * block_rows
    state_now, unused = lax.scan(visit, state_now, (prefix_keys, prefix_vals, starts))
    run_max, run_sum, run_acc = state_now
    result = run_acc / run_sum[..., None]
    result = result.transpose(2, 0, 1, 3).reshape(1, suffix_rows, kv_local * group * HEAD_DIM)
    return result.astype(jnp.bfloat16)


def solution(mesh):
    in_specs = (
        P(("groups", "replica"), None, "tensor"),
        P(("groups", "replica"), None, None, "tensor"),
        P(("groups", "replica"), None, "tensor", None),
        P("groups", None),
        P("groups", None),
        P("groups"),
    )
    out_specs = P(("groups", "replica"), None, "tensor")
    return jax.shard_map(
        on_device, mesh=mesh, in_specs=in_specs, out_specs=out_specs, check_vma=False
    )
```

profile of v0, /device:TPU:9, one launch (start us, length us, event | category | flops | bytes accessed | tf_op | source)
XLA Modules:
  0.0 132.8 jit_solution(631455684307266697)
XLA Ops:
  0.0 12.7 %copy.73 = bf16[12,2,32,1024]{2,0,1,3:T(8,128)(2,1)} copy(bf16[12,2,32,1024]{3,2,1,0:T(8,128)(2,1)} %param.12) | data formatting | bytes 3145728 | tf_op args[2]
  12.7 8.9 %reshape.178 = bf16[4,2,98304]{2,1,0:T(2,128)(2,1)} reshape(bf16[1024,2,12,32]{3,2,1,0:T(8,128)(2,1)} %bitcast.95) | data formatting | bytes 3145728
  21.6 4.3 %all-to-all-start = ((bf16[4,2,98304]{2,1,0:T(2,128)(2,1)}), bf16[4,2,98304]{2,1,0:T(2,128)(2,1)S(1)}, u32[]{:S(2)}, u32[]{:S(2)}) async-start(bf16[4,2,98304]{2,1,0:T(2,128)(2,1)} %reshape.178), calls=%async_computation | async-start | bytes 3145728 | tf_op jit(solution)/shard_map/all_to_all | solution.py:64
  29.1 16.0 %all-to-all-done = bf16[4,2,98304]{2,1,0:T(2,128)(2,1)S(1)} async-done(((bf16[4,2,98304]{2,1,0:T(2,128)(2,1)}), bf16[4,2,98304]{2,1,0:T(2,128)(2,1)S(1)}, u32[]{:S(2)}, u32[]{:S(2)}) %all-to-all-start) | async-done | bytes 1572896 | tf_op jit(solution)/shard_map/all_to_all | solution.py:64
  45.1 7.1 %reshape.179 = bf16[1024,2,12,32]{3,2,1,0:T(8,128)(2,1)} reshape(bf16[4,2,98304]{2,1,0:T(2,128)(2,1)S(1)} %all-to-all-done) | data formatting | bytes 3145728
  52.2 9.6 %copy.91 = bf16[12,2,32,4,256]{4,3,2,1,0:T(4,128)(2,1)S(1)} copy(bf16[12,2,32,4,256]{2,0,1,4,3:T(8,128)(2,1)} %bitcast.94) | data formatting | bytes 3145728 | tf_op jit(solution)/shard_map/all_to_all | solution.py:64
  61.7 1.5 %copy.75 = bf16[12,2,4,32,256]{4,3,2,1,0:T(8,128)(2,1)} copy(bf16[12,2,4,32,256]{4,2,3,1,0:T(4,128)(2,1)S(1)} %bitcast.96) | data formatting | bytes 3145728 | tf_op jit(solution)/shard_map/all_to_all | solution.py:64
  63.2 2.1 %gather_fusion = bf16[12,2,128,256]{3,2,1,0:T(8,128)(2,1)S(1)} fusion(bf16[12,2,128,256]{3,2,1,0:T(8,128)(2,1)} %bitcast.97, s32[1024]{0:T(1024)S(1)} %pad_clamp_fusion.1), kind=kCustom, calls=%fused_computation.2 | custom fusion | bytes 3145776 | tf_op jit(solution)/shard_map/jit(_take)/gather | solution.py:43
  65.5 1.1 fusion.35
  66.6 1.3 collective-permute-start
  68.9 1.5 %collective-permute-start.2 = (bf16[4,2,128,256]{3,2,1,0:T(8,128)(2,1)S(1)}, bf16[4,2,128,256]{3,2,1,0:T(8,128)(2,1)}, u32[]{:S(2)}, u32[]{:S(2)}) collective-permute-start(bf16[4,2,128,256]{3,2,1,0:T(8,128)(2,1)S(1)} %get-tuple-element.151), channel_id=1, source_target_pairs={{0,12},{4,0},{8,4},{12,8},{1,13},{5,1},{9,5},{13,9},{2,14},{6,2},{... | collective-permute-start | bytes 1572872 | tf_op jit(solution)/shard_map/ppermute | solution.py:16
  71.4 1.5 %convolution_add_fusion = f32[2,8,128,128]{3,2,1,0:T(8,128)} fusion(bf16[128,2,128,1]{0,2,3,1:T(8,128)(2,1)S(1)} %bitcast.102, f32[2,8,128,128]{2,3,1,0:T(8,128)S(1)} %get-tuple-element.160, f32[2,8,128]{2,1,0:T(8,128)S(1)} %get-tuple-element.157, f32[2,8,128]{2,1,0:T(8,128)S(1)} %broadcast_maximum_fusion, pred[128,128]{0,1:T(8,128)(4,1)S(1)} %iota_compare_fusion), kind=kOutput, calls=%fused_computation.30 | convolution fusion | flops 68157440 | bytes 2195456 | tf_op jit(solution)/shard_map/kgqc,ckd->kgqd/dot_general | solution.py:26
  72.9 6.5 %collective-permute-done = bf16[4,2,128,256]{3,2,1,0:T(8,128)(2,1)S(1)} collective-permute-done((bf16[4,2,128,256]{3,2,1,0:T(8,128)(2,1)}, bf16[4,2,128,256]{3,2,1,0:T(8,128)(2,1)S(1)}, u32[]{:S(2)}, u32[]{:S(2)}) %collective-permute-start) | collective-permute-done | bytes 524320 | tf_op jit(solution)/shard_map/ppermute | solution.py:16
  79.4 32.9 %collective-permute-done.1 = bf16[4,2,128,256]{3,2,1,0:T(8,128)(2,1)} collective-permute-done((bf16[4,2,128,256]{3,2,1,0:T(8,128)(2,1)}, bf16[4,2,128,256]{3,2,1,0:T(8,128)(2,1)}, u32[]{:S(2)}, u32[]{:S(2)}) %collective-permute-start.1) | collective-permute-done | bytes 524320 | tf_op jit(solution)/shard_map/ppermute | solution.py:16
  112.3 3.1 %collective-permute-done.2 = bf16[4,2,128,256]{3,2,1,0:T(8,128)(2,1)} collective-permute-done((bf16[4,2,128,256]{3,2,1,0:T(8,128)(2,1)S(1)}, bf16[4,2,128,256]{3,2,1,0:T(8,128)(2,1)}, u32[]{:S(2)}, u32[]{:S(2)}) %collective-permute-start.2) | collective-permute-done | bytes 524320 | tf_op jit(solution)/shard_map/ppermute | solution.py:16
  115.4 1.5 %pad_maximum_fusion = bf16[3,4,2,128,256]{4,3,2,1,0:T(8,128)(2,1)S(1)} fusion(bf16[1,4,2,128,256]{4,3,2,1,0:T(8,128)(2,1)} %bitcast.14, bf16[1,4,2,128,256]{4,3,2,1,0:T(8,128)(2,1)} %bitcast.13, bf16[1,4,2,128,256]{4,3,2,1,0:T(8,128)(2,1)} %bitcast.101), kind=kLoop, calls=%fused_computation.28 | loop fusion | flops 1572864 | bytes 3145728 | tf_op jit(solution)/shard_map/stack | solution.py:69
  118.9 12.1 %while.15 = (s32[]{:T(128)}, f32[2,8,128]{2,1,0:T(8,128)S(1)}, f32[2,8,128]{2,1,0:T(8,128)S(1)}, f32[2,8,128,128]{3,2,1,0:T(8,128)S(1)}, s32[2]{0:T(128)S(1)}, /...) while((s32[]{:T(128)}, f32[2,8,128]{2,1,0:T(8,128)S(1)}, ...), condition=%wide.region_8.10_spmd.clone, body=%wide.region_5.9_spmd.clone.sunk | while | flops 551031808 | bytes 16910460 | solution.py:111
  119.5 1.2 fusion.50
  121.9 1.1 fusion.51
  123.1 1.9 %fusion.52 = f32[2,8,128,128]{3,2,1,0:T(8,128)S(1)} fusion(f32[2,512,128,8]{2,1,3,0:T(8,128)S(1)} %get-tuple-element.226, f32[2,8,128]{2,1,0:T(8,128)S(1)} %max.5, pred[512]{0:T(512)(128)(4,1)S(1)} %fusion.50, f32[2,8,128,128]{3,2,1,0:T(8,128)S(1)} %get-tuple-element.243, f32[2,8,128]{2,1,0:T(8,128)S(1)} %get-tuple-element.228, ...), kind=kOutput, calls=%fused_computation.15.clone.1 | convolution fusion | flops 274202624 | bytes 6570496 | tf_op jit(solution)/shard_map/while/body/eval_jaxpr/kgqc,ckd->kgqd/dot_general | solution.py:26
  125.6 1.2 fusion.50
  127.9 1.1 fusion.51
  129.1 1.9 %fusion.52 = f32[2,8,128,128]{3,2,1,0:T(8,128)S(1)} fusion(f32[2,512,128,8]{2,1,3,0:T(8,128)S(1)} %get-tuple-element.226, f32[2,8,128]{2,1,0:T(8,128)S(1)} %max.5, pred[512]{0:T(512)(128)(4,1)S(1)} %fusion.50, f32[2,8,128,128]{3,2,1,0:T(8,128)S(1)} %get-tuple-element.243, f32[2,8,128]{2,1,0:T(8,128)S(1)} %get-tuple-element.228, ...), kind=kOutput, calls=%fused_computation.15.clone.1 | convolution fusion | flops 274202624 | bytes 6570496 | tf_op jit(solution)/shard_map/while/body/eval_jaxpr/kgqc,ckd->kgqd/dot_general | solution.py:26
  131.7 1.0 convert_element_type.35
  (67 shorter events, 11.4 us)
Async XLA Ops:
  0.0 26.5 %copy-start = (s32[4,8]{1,0:T(4,128)S(1)}, s32[4,8]{1,0:T(4,128)}, u32[]{:S(2)}) copy-start(s32[4,8]{1,0:T(4,128)} %param.14) | copy-start | bytes 388
  12.7 13.3 %copy-start.4 = (s32[4,8]{1,0:T(4,128)S(1)}, s32[4,8]{1,0:T(4,128)}, u32[]{:S(2)}) copy-start(s32[4,8]{1,0:T(4,128)} %param.13) | copy-start | bytes 388
  12.7 15.3 %copy-start.2 = (bf16[1,128,2048]{2,1,0:T(8,128)(2,1)S(1)}, bf16[1,128,2048]{2,1,0:T(8,128)(2,1)}, u32[]{:S(2)}) copy-start(bf16[1,128,2048]{2,1,0:T(8,128)(2,1)} %param.10) | copy-start | bytes 1572868
  21.6 6.7 %copy-start.5 = (bf16[1,2,128,256]{3,2,1,0:T(8,128)(2,1)S(1)}, bf16[1,2,128,256]{3,2,1,0:T(8,128)(2,1)}, u32[]{:S(2)}) copy-start(bf16[1,2,128,256]{3,2,1,0:T(8,128)(2,1)} %param.11) | copy-start | bytes 393220
  21.6 23.6 %all-to-all-start = ((bf16[4,2,98304]{2,1,0:T(2,128)(2,1)}), bf16[4,2,98304]{2,1,0:T(2,128)(2,1)S(1)}, u32[]{:S(2)}, u32[]{:S(2)}) async-start(bf16[4,2,98304]{2,1,0:T(2,128)(2,1)} %reshape.178), calls=%async_computation | async-start | bytes 3145728 | tf_op jit(solution)/shard_map/all_to_all | solution.py:64
  65.3 5.5 %copy-start.6 = (s32[4]{0:T(128)S(1)}, s32[4]{0:T(128)}, u32[]{:S(2)}) copy-start(s32[4]{0:T(128)} %param.15) | copy-start | bytes 52
  66.6 12.8 %collective-permute-start = (bf16[4,2,128,256]{3,2,1,0:T(8,128)(2,1)}, bf16[4,2,128,256]{3,2,1,0:T(8,128)(2,1)S(1)}, u32[]{:S(2)}, u32[]{:S(2)}) collective-permute-start(bf16[4,2,128,256]{3,2,1,0:T(8,128)(2,1)} %get-tuple-element.150), channel_id=1, source_target_pairs={{0,4},{4,8},{8,12},{12,0},{1,5},{5,9},{9,13},{13,1},{2,6},{6,10},{... | collective-permute-start | bytes 1572872 | tf_op jit(solution)/shard_map/ppermute | solution.py:16
  67.9 44.4 %collective-permute-start.1 = (bf16[4,2,128,256]{3,2,1,0:T(8,128)(2,1)}, bf16[4,2,128,256]{3,2,1,0:T(8,128)(2,1)}, u32[]{:S(2)}, u32[]{:S(2)}) collective-permute-start(bf16[4,2,128,256]{3,2,1,0:T(8,128)(2,1)} %get-tuple-element.152), channel_id=1, source_target_pairs={{0,8},{4,12},{8,0},{12,4},{1,9},{5,13},{9,1},{13,5},{2,10},{6,14},... | collective-permute-start | bytes 1572872 | tf_op jit(solution)/shard_map/ppermute | solution.py:16
  68.9 46.4 %collective-permute-start.2 = (bf16[4,2,128,256]{3,2,1,0:T(8,128)(2,1)S(1)}, bf16[4,2,128,256]{3,2,1,0:T(8,128)(2,1)}, u32[]{:S(2)}, u32[]{:S(2)}) collective-permute-start(bf16[4,2,128,256]{3,2,1,0:T(8,128)(2,1)S(1)} %get-tuple-element.151), channel_id=1, source_target_pairs={{0,12},{4,0},{8,4},{12,8},{1,13},{5,1},{9,5},{13,9},{2,14},{6,2},{... | collective-permute-start | bytes 1572872 | tf_op jit(solution)/shard_map/ppermute | solution.py:16
  79.4 36.0 %copy-start.3 = (bf16[4,2,128,256]{3,2,1,0:T(8,128)(2,1)}, bf16[4,2,128,256]{3,2,1,0:T(8,128)(2,1)S(1)}, u32[]{:S(2)}) copy-start(bf16[4,2,128,256]{3,2,1,0:T(8,128)(2,1)S(1)} %collective-permute-done) | copy-start | bytes 1572868
  117.7 1.2 copy-start.1
where the time goes:
time: 133 us
  waiting for transfers between devices  58.5 us (44%)
  local copies, waits for them, and re-layouts  50.6 us (38%)
  starting transfers between devices  8.11 us (6%)
  other arithmetic  7.99 us (6%)
  matrix products  7.18 us (5%)
    ppermute x3, waiting for transfers between devices, passed_along(): return lax.ppermute(value, axis, pairs)  42.4 us
    unnamed x21, local copies, waits for them, and re-layouts  30.3 us
    all_to_all x1, waiting for transfers between devices, on_device(): lax.all_to_all(page_pool, 'tensor', split_axis=3, concat_axis=2, tiled=True)  16 us
    all_to_all x2, local copies, waits for them, and re-layouts, on_device(): lax.all_to_all(page_pool, 'tensor', split_axis=3, concat_axis=2, tiled=True)  11 us
    dot_general x3, matrix products, absorb(): jnp.einsum('kgqc,ckd->kgqd', weights.astype(jnp.bfloat16), values, prefer...  5.31 us
    all_to_all x1, starting transfers between devices, on_device(): lax.all_to_all(page_pool, 'tensor', split_axis=3, concat_axis=2, tiled=True)  4.34 us
    ppermute x3, starting transfers between devices, passed_along(): return lax.ppermute(value, axis, pairs)  3.78 us
  transfers between devices with their start and end apart: 4, of which 4 were waited for; matrix products, arithmetic and copies ran while one was open for 4% of the time, Pallas kernels for 0%

commit v1 on v0

--- a/solution.py
+++ b/solution.py
@@ -61,7 +61,25 @@
     slot_cap = (page_count + span_count - 1) // span_count + 1
     own_offsets = lax.dynamic_index_in_dim(offsets, reader, 0, keepdims=False)
     own_length = lax.dynamic_index_in_dim(prefix_len, reader, 0, keepdims=False)
-    source = lax.all_to_all(page_pool, "tensor", split_axis=3, concat_axis=2, tiled=True)
+    inter = lax.axis_size("tensor")
+    far_arr = lax.axis_index("tensor")
+    row_out, current_value = (inter, far_arr)
+    t_next = page_pool.shape[3] // row_out
+    block_next = list(page_pool.shape)
+    block_next[3] = t_next
+    y_new = block_next[2]
+    block_next[2] = y_new * row_out
+    source = jnp.zeros(block_next, page_pool.dtype)
+    for dev in range(row_out):
+        a_now = lax.dynamic_slice_in_dim(page_pool, (current_value ^ dev) * t_next, t_next, axis=3)
+        if dev:
+            all_blocks = []
+            for kk in range(row_out):
+                all_blocks.append((kk, kk ^ dev))
+            a_now = lax.ppermute(a_now, axis_name="tensor", perm=all_blocks)
+        source = lax.dynamic_update_slice_in_dim(
+            source, a_now, (current_value ^ dev) * y_new, axis=2
+        )
     payload = pack_pages(source, offsets, slots, reader, replicas, span_count, slot_cap)
     arrivals = []
     for distance in range(1, span_count + 1):

time: 133 us -> 98.6 us (0.74)
  the two profiles are of different devices: /device:TPU:9 before, /device:TPU:0 now
where the time goes in v1:
time: 98.6 us; the launch traced here: 98 us
  waiting for transfers between devices  46.7 us (47%)
  local copies, waits for them, and re-layouts  20.4 us (21%)
  other arithmetic  13.9 us (14%)
  starting transfers between devices  8.48 us (9%)
  matrix products  8.03 us (8%)
    ppermute x3, waiting for transfers between devices, passed_along(): return lax.ppermute(value, axis, pairs)  42.5 us
    ppermute x3, starting transfers between devices, passed_along(): return lax.ppermute(value, axis, pairs)  5.43 us
    dot_general x3, matrix products, absorb(): jnp.einsum('kgqc,ckd->kgqd', weights.astype(jnp.bfloat16), values, prefer...  5.32 us
    unnamed x28, local copies, waits for them, and re-layouts  5.27 us
    ppermute x3, waiting for transfers between devices, on_device(): a_now = lax.ppermute(a_now, axis_name='tensor', perm=all_blocks)  4.17 us
    reduce_sum x3, other arithmetic, absorb(): run_sum = run_sum * rescale + jnp.sum(weights, axis=-1)  3.86 us
    dynamic_update_slice x3, local copies, waits for them, and re-layouts, on_device(): lax.dynamic_update_slice_in_dim(source, a_now, (current_value ^ dev) * y_...  3.08 us
    ppermute x3, starting transfers between devices, on_device(): a_now = lax.ppermute(a_now, axis_name='tensor', perm=all_blocks)  3.06 us
  transfers between devices with their start and end apart: 6, of which 4 were waited for; matrix products, arithmetic and copies ran while one was open for 17% of the time, Pallas kernels for 0%

profile of v1, /device:TPU:0, one launch (start us, length us, event | category | flops | bytes accessed | tf_op | source)
XLA Modules:
  0.0 98.0 jit_solution(15418257391009124400)
XLA Ops:
  0.2 1.3 %copy-done.2 = bf16[12,2,32,1024]{3,2,1,0:T(8,128)(2,1)S(1)} copy-done((bf16[12,2,32,1024]{3,2,1,0:T(8,128)(2,1)S(1)}, bf16[12,2,32,1024]{3,2,1,0:T(8,128)(2,1)}, u32[]{:S(2)}) %copy-start.2) | copy-done | bytes 1572888
  2.5 2.4 %collective-permute-start.2 = (bf16[12,2,32,256]{3,2,1,0:T(8,128)(2,1)S(1)}, bf16[12,2,32,256]{3,2,1,0:T(8,128)(2,1)}, u32[]{:S(2)}, u32[]{:S(2)}) collective-permute-start(bf16[12,2,32,256]{3,2,1,0:T(8,128)(2,1)S(1)} %get-tuple-element.135), channel_id=1, source_target_pairs={{0,3},{1,2},{2,1},{3,0},{4,7},{5,6},{6,5},{7,4},{8,11},{9,10},{10,... | collective-permute-start | bytes 1179656 | tf_op jit(solution)/shard_map/ppermute | solution.py:79
  9.8 1.5 %fusion.37 = (bf16[1,1,128,256]{3,2,1,0:T(8,128)(2,1)}, bf16[1,1,128,256]{3,2,1,0:T(8,128)(2,1)S(1)}) fusion(bf16[1,2,128,256]{3,2,1,0:T(8,128)(2,1)} %param.11), kind=kLoop, calls=%fused_computation.88 | loop fusion | bytes 262144 | tf_op jit(solution)/shard_map/slice | solution.py:98
  12.1 1.3 %copy.36 = bf16[1,128,2048]{1,2,0:T(8,128)(2,1)S(1)} copy(bf16[1,128,2048]{2,1,0:T(8,128)(2,1)} %param.10) | data formatting | bytes 1048576 | tf_op args[0]
  13.4 1.2 %fusion.38 = (f32[2,8,128]{2,1,0:T(8,128)S(1)}, f32[2,8,128,128]{2,3,1,0:T(8,128)S(1)}) fusion(bf16[128,2,128,1]{0,2,3,1:T(8,128)(2,1)} %bitcast.95, bf16[128,2,8,128]{0,3,2,1:T(8,128)(2,1)S(1)} %bitcast.89, pred[128,128]{0,1:T(8,128)(4,1)} %iota_compare_fusion), kind=kOutput, calls=%fused_computation.89 | convolution fusion | flops 67893248 | bytes 1662976 | tf_op jit(solution)/shard_map/qkgd,ckd->kgqc/dot_general | solution.py:105
  16.4 1.5 %fusion.21 = f32[2,8,128]{2,1,0:T(8,128)} fusion(f32[2,8,128,128]{2,3,1,0:T(8,128)S(1)} %get-tuple-element.146, f32[2,8,128]{2,1,0:T(8,128)S(1)} %broadcast_maximum_fusion, pred[128,128]{0,1:T(8,128)(4,1)} %iota_compare_fusion), kind=kLoop, calls=%fused_computation.38 | loop fusion | flops 784384 | bytes 1081344 | tf_op jit(solution)/shard_map/reduce_sum | solution.py:25
  18.9 4.2 %collective-permute-done.1 = bf16[12,2,32,256]{3,2,1,0:T(8,128)(2,1)} collective-permute-done((bf16[12,2,32,256]{3,2,1,0:T(8,128)(2,1)}, bf16[12,2,32,256]{3,2,1,0:T(8,128)(2,1)}, u32[]{:S(2)}, u32[]{:S(2)}) %collective-permute-start.1) | collective-permute-done | bytes 393248 | tf_op jit(solution)/shard_map/ppermute | solution.py:79
  25.2 2.0 %gather_fusion = bf16[12,2,128,256]{3,2,1,0:T(8,128)(2,1)} fusion(bf16[12,2,128,256]{3,2,1,0:T(8,128)(2,1)S(1)} %constant_dynamic-update-slice_fusion, s32[1024]{0:T(1024)} %pad_clamp_fusion.1), kind=kCustom, calls=%fused_computation.2 | custom fusion | bytes 3145776 | tf_op jit(solution)/shard_map/jit(_take)/gather | solution.py:43
  27.2 1.6 %broadcast_select_fusion = bf16[12,2,128,256]{3,2,1,0:T(8,128)(2,1)S(1)} fusion(bf16[12,2,128,256]{3,2,1,0:T(8,128)(2,1)} %gather_fusion, pred[12]{0:T(512)(128)(4,1)S(1)} %copy-done.10), kind=kLoop, calls=%fused_computation.29 | loop fusion | flops 786432 | bytes 3145740 | tf_op jit(solution)/shard_map/jit(_take)/select_n | solution.py:43
  28.8 1.2 %fusion.35 = (bf16[4,2,128,256]{3,2,1,0:T(8,128)(2,1)}, bf16[4,2,128,256]{3,2,1,0:T(8,128)(2,1)}, bf16[4,2,128,256]{3,2,1,0:T(8,128)(2,1)}) fusion(bf16[12,2,128,256]{3,2,1,0:T(8,128)(2,1)S(1)} %broadcast_select_fusion), kind=kLoop, calls=%fused_computation.86 | loop fusion | bytes 3145728 | tf_op jit(solution)/shard_map/slice | solution.py:86
  30.0 2.4 %collective-permute-start.3 = (bf16[4,2,128,256]{3,2,1,0:T(8,128)(2,1)}, bf16[4,2,128,256]{3,2,1,0:T(8,128)(2,1)S(1)}, u32[]{:S(2)}, u32[]{:S(2)}) collective-permute-start(bf16[4,2,128,256]{3,2,1,0:T(8,128)(2,1)} %get-tuple-element.132), channel_id=1, source_target_pairs={{0,4},{4,8},{8,12},{12,0},{1,5},{5,9},{9,13},{13,1},{2,6},{6,10},{... | collective-permute-start | bytes 1572872 | tf_op jit(solution)/shard_map/ppermute | solution.py:16
  32.4 2.0 %collective-permute-start.5 = (bf16[4,2,128,256]{3,2,1,0:T(8,128)(2,1)}, bf16[4,2,128,256]{3,2,1,0:T(8,128)(2,1)S(1)}, u32[]{:S(2)}, u32[]{:S(2)}) collective-permute-start(bf16[4,2,128,256]{3,2,1,0:T(8,128)(2,1)} %get-tuple-element.133), channel_id=1, source_target_pairs={{0,12},{4,0},{8,4},{12,8},{1,13},{5,1},{9,5},{13,9},{2,14},{6,2},{... | collective-permute-start | bytes 1572872 | tf_op jit(solution)/shard_map/ppermute | solution.py:16
  36.6 1.5 %convolution_add_fusion = f32[2,8,128,128]{3,2,1,0:T(8,128)} fusion(bf16[128,2,128,1]{0,2,3,1:T(8,128)(2,1)S(1)} %bitcast.94, f32[2,8,128,128]{2,3,1,0:T(8,128)S(1)} %get-tuple-element.146, f32[2,8,128]{2,1,0:T(8,128)S(1)} %get-tuple-element.143, f32[2,8,128]{2,1,0:T(8,128)S(1)} %broadcast_maximum_fusion, pred[128,128]{0,1:T(8,128)(4,1)S(1)} %copy-done.3), kind=kOutput, calls=%fused_computation.30 | convolution fusion | flops 68157440 | bytes 2195456 | tf_op jit(solution)/shard_map/kgqc,ckd->kgqd/dot_general | solution.py:26
  38.1 9.3 %collective-permute-done.3 = bf16[4,2,128,256]{3,2,1,0:T(8,128)(2,1)S(1)} collective-permute-done((bf16[4,2,128,256]{3,2,1,0:T(8,128)(2,1)}, bf16[4,2,128,256]{3,2,1,0:T(8,128)(2,1)S(1)}, u32[]{:S(2)}, u32[]{:S(2)}) %collective-permute-start.3) | collective-permute-done | bytes 524320 | tf_op jit(solution)/shard_map/ppermute | solution.py:16
  47.4 10.1 %collective-permute-done.5 = bf16[4,2,128,256]{3,2,1,0:T(8,128)(2,1)S(1)} collective-permute-done((bf16[4,2,128,256]{3,2,1,0:T(8,128)(2,1)}, bf16[4,2,128,256]{3,2,1,0:T(8,128)(2,1)S(1)}, u32[]{:S(2)}, u32[]{:S(2)}) %collective-permute-start.5) | collective-permute-done | bytes 524320 | tf_op jit(solution)/shard_map/ppermute | solution.py:16
  57.5 23.1 %collective-permute-done.4 = bf16[4,2,128,256]{3,2,1,0:T(8,128)(2,1)} collective-permute-done((bf16[4,2,128,256]{3,2,1,0:T(8,128)(2,1)}, bf16[4,2,128,256]{3,2,1,0:T(8,128)(2,1)}, u32[]{:S(2)}, u32[]{:S(2)}) %collective-permute-start.4) | collective-permute-done | bytes 524320 | tf_op jit(solution)/shard_map/ppermute | solution.py:16
  80.6 1.2 %pad_maximum_fusion = bf16[3,4,2,128,256]{4,3,2,1,0:T(8,128)(2,1)S(1)} fusion(bf16[1,4,2,128,256]{4,3,2,1,0:T(8,128)(2,1)S(1)} %bitcast.93, bf16[1,4,2,128,256]{4,3,2,1,0:T(8,128)(2,1)} %bitcast.10, bf16[1,4,2,128,256]{4,3,2,1,0:T(8,128)(2,1)S(1)} %bitcast.92), kind=kLoop, calls=%fused_computation.28 | loop fusion | flops 1572864 | bytes 3145728 | tf_op jit(solution)/shard_map/stack | solution.py:87
  84.0 12.3 %while.15 = (s32[]{:T(128)}, f32[2,8,128]{2,1,0:T(8,128)S(1)}, f32[2,8,128]{2,1,0:T(8,128)S(1)}, f32[2,8,128,128]{3,2,1,0:T(8,128)S(1)}, s32[2]{0:T(128)S(1)}, /...) while((s32[]{:T(128)}, f32[2,8,128]{2,1,0:T(8,128)S(1)}, ...), condition=%wide.region_8.10_spmd.clone, body=%wide.region_5.9_spmd.clone.sunk | while | flops 551031808 | bytes 16910468 | solution.py:129
  84.5 1.3 %fusion.50 = pred[512]{0:T(512)(128)(4,1)S(1)} fusion(s32[]{:T(128)} %get-tuple-element.241, s32[]{:T(128)} %bitcast.88), kind=kLoop, calls=%fused_computation.22.clone.1 | loop fusion | flops 1024 | bytes 520 | tf_op jit(solution)/shard_map/while/body/eval_jaxpr/lt | solution.py:125
  87.0 1.2 %fusion.51 = f32[2,8,128]{2,1,0:T(8,128)S(1)} fusion(f32[2,512,128,8]{2,1,3,0:T(8,128)S(1)} %get-tuple-element.212, f32[2,8,128]{2,1,0:T(8,128)S(1)} %max.5, pred[512]{0:T(512)(128)(4,1)S(1)} %fusion.50), kind=kLoop, calls=%fused_computation.11.clone.1 | loop fusion | flops 5240832 | bytes 4211200 | tf_op jit(solution)/shard_map/while/body/eval_jaxpr/reduce_sum | solution.py:25
  88.2 1.9 %fusion.52 = f32[2,8,128,128]{3,2,1,0:T(8,128)S(1)} fusion(f32[2,512,128,8]{2,1,3,0:T(8,128)S(1)} %get-tuple-element.212, f32[2,8,128]{2,1,0:T(8,128)S(1)} %max.5, pred[512]{0:T(512)(128)(4,1)S(1)} %fusion.50, f32[2,8,128,128]{3,2,1,0:T(8,128)S(1)} %get-tuple-element.229, f32[2,8,128]{2,1,0:T(8,128)S(1)} %get-tuple-element.214, ...), kind=kOutput, calls=%fused_computation.15.clone.1 | convolution fusion | flops 274202624 | bytes 6570496 | tf_op jit(solution)/shard_map/while/body/eval_jaxpr/kgqc,ckd->kgqd/dot_general | solution.py:26
  90.7 1.3 %fusion.50 = pred[512]{0:T(512)(128)(4,1)S(1)} fusion(s32[]{:T(128)} %get-tuple-element.241, s32[]{:T(128)} %bitcast.88), kind=kLoop, calls=%fused_computation.22.clone.1 | loop fusion | flops 1024 | bytes 520 | tf_op jit(solution)/shard_map/while/body/eval_jaxpr/lt | solution.py:125
  93.1 1.2 %fusion.51 = f32[2,8,128]{2,1,0:T(8,128)S(1)} fusion(f32[2,512,128,8]{2,1,3,0:T(8,128)S(1)} %get-tuple-element.212, f32[2,8,128]{2,1,0:T(8,128)S(1)} %max.5, pred[512]{0:T(512)(128)(4,1)S(1)} %fusion.50), kind=kLoop, calls=%fused_computation.11.clone.1 | loop fusion | flops 5240832 | bytes 4211200 | tf_op jit(solution)/shard_map/while/body/eval_jaxpr/reduce_sum | solution.py:25
  94.3 1.9 %fusion.52 = f32[2,8,128,128]{3,2,1,0:T(8,128)S(1)} fusion(f32[2,512,128,8]{2,1,3,0:T(8,128)S(1)} %get-tuple-element.212, f32[2,8,128]{2,1,0:T(8,128)S(1)} %max.5, pred[512]{0:T(512)(128)(4,1)S(1)} %fusion.50, f32[2,8,128,128]{3,2,1,0:T(8,128)S(1)} %get-tuple-element.229, f32[2,8,128]{2,1,0:T(8,128)S(1)} %get-tuple-element.214, ...), kind=kOutput, calls=%fused_computation.15.clone.1 | convolution fusion | flops 274202624 | bytes 6570496 | tf_op jit(solution)/shard_map/while/body/eval_jaxpr/kgqc,ckd->kgqd/dot_general | solution.py:26
  (81 shorter events, 21.1 us)
Async XLA Ops:
  0.0 7.4 %copy-start = (s32[4,8]{1,0:T(4,128)S(1)}, s32[4,8]{1,0:T(4,128)}, u32[]{:S(2)}) copy-start(s32[4,8]{1,0:T(4,128)} %param.14) | copy-start | bytes 388
  0.0 1.4 %copy-start.2 = (bf16[12,2,32,1024]{3,2,1,0:T(8,128)(2,1)S(1)}, bf16[12,2,32,1024]{3,2,1,0:T(8,128)(2,1)}, u32[]{:S(2)}) copy-start(bf16[12,2,32,1024]{3,2,1,0:T(8,128)(2,1)} %param.12) | copy-start | bytes 4718596
  1.4 4.2 %copy-start.5 = (s32[4,8]{1,0:T(4,128)S(1)}, s32[4,8]{1,0:T(4,128)}, u32[]{:S(2)}) copy-start(s32[4,8]{1,0:T(4,128)} %param.13) | copy-start | bytes 388
  2.5 21.6 %collective-permute-start.2 = (bf16[12,2,32,256]{3,2,1,0:T(8,128)(2,1)S(1)}, bf16[12,2,32,256]{3,2,1,0:T(8,128)(2,1)}, u32[]{:S(2)}, u32[]{:S(2)}) collective-permute-start(bf16[12,2,32,256]{3,2,1,0:T(8,128)(2,1)S(1)} %get-tuple-element.135), channel_id=1, source_target_pairs={{0,3},{1,2},{2,1},{3,0},{4,7},{5,6},{6,5},{7,4},{8,11},{9,10},{10,... | collective-permute-start | bytes 1179656 | tf_op jit(solution)/shard_map/ppermute | solution.py:79
  4.9 13.0 %collective-permute-start = (bf16[12,2,32,256]{3,2,1,0:T(8,128)(2,1)}, bf16[12,2,32,256]{3,2,1,0:T(8,128)(2,1)}, u32[]{:S(2)}, u32[]{:S(2)}) collective-permute-start(bf16[12,2,32,256]{3,2,1,0:T(8,128)(2,1)} %get-tuple-element.136), channel_id=1, source_target_pairs={{0,1},{1,0},{2,3},{3,2},{4,5},{5,4},{6,7},{7,6},{8,9},{9,8},{10,11... | collective-permute-start | bytes 1179656 | tf_op jit(solution)/shard_map/ppermute | solution.py:79
  5.6 17.5 %collective-permute-start.1 = (bf16[12,2,32,256]{3,2,1,0:T(8,128)(2,1)}, bf16[12,2,32,256]{3,2,1,0:T(8,128)(2,1)}, u32[]{:S(2)}, u32[]{:S(2)}) collective-permute-start(bf16[12,2,32,256]{3,2,1,0:T(8,128)(2,1)} %get-tuple-element.138), channel_id=1, source_target_pairs={{0,2},{1,3},{2,0},{3,1},{4,6},{5,7},{6,4},{7,5},{8,10},{9,11},{10,... | collective-permute-start | bytes 1179656 | tf_op jit(solution)/shard_map/ppermute | solution.py:79
  14.6 0.6 copy-start.6
  25.2 2.0 %copy-start.10 = (pred[12]{0:T(512)(128)(4,1)S(1)}, pred[12]{0:T(512)(128)(4,1)}, u32[]{:S(2)}) copy-start(pred[12]{0:T(512)(128)(4,1)} %compare_and_fusion.1) | copy-start | bytes 40
  28.8 7.0 %copy-start.11 = (s32[4]{0:T(128)S(1)}, s32[4]{0:T(128)}, u32[]{:S(2)}) copy-start(s32[4]{0:T(128)} %param.15) | copy-start | bytes 52
  28.8 7.6 %copy-start.4 = (bf16[1,1,128,256]{3,2,1,0:T(8,128)(2,1)S(1)}, bf16[1,1,128,256]{3,2,1,0:T(8,128)(2,1)}, u32[]{:S(2)}) copy-start(bf16[1,1,128,256]{3,2,1,0:T(8,128)(2,1)} %get-tuple-element.141) | copy-start | bytes 196612
  28.8 7.7 %copy-start.7 = (f32[2,8,128]{2,1,0:T(8,128)S(1)}, f32[2,8,128]{2,1,0:T(8,128)}, u32[]{:S(2)}) copy-start(f32[2,8,128]{2,1,0:T(8,128)} %copy-done.6) | copy-start | bytes 24580
  28.8 7.7 %copy-start.8 = (f32[2,8,128]{2,1,0:T(8,128)S(1)}, f32[2,8,128]{2,1,0:T(8,128)}, u32[]{:S(2)}) copy-start(f32[2,8,128]{2,1,0:T(8,128)} %fusion.21) | copy-start | bytes 24580
  28.8 7.7 %copy-start.3 = (pred[128,128]{0,1:T(8,128)(4,1)S(1)}, pred[128,128]{0,1:T(8,128)(4,1)}, u32[]{:S(2)}) copy-start(pred[128,128]{0,1:T(8,128)(4,1)} %iota_compare_fusion) | copy-start | bytes 49156
  30.0 17.4 %collective-permute-start.3 = (bf16[4,2,128,256]{3,2,1,0:T(8,128)(2,1)}, bf16[4,2,128,256]{3,2,1,0:T(8,128)(2,1)S(1)}, u32[]{:S(2)}, u32[]{:S(2)}) collective-permute-start(bf16[4,2,128,256]{3,2,1,0:T(8,128)(2,1)} %get-tuple-element.132), channel_id=1, source_target_pairs={{0,4},{4,8},{8,12},{12,0},{1,5},{5,9},{9,13},{13,1},{2,6},{6,10},{... | collective-permute-start | bytes 1572872 | tf_op jit(solution)/shard_map/ppermute | solution.py:16
  32.4 25.1 %collective-permute-start.5 = (bf16[4,2,128,256]{3,2,1,0:T(8,128)(2,1)}, bf16[4,2,128,256]{3,2,1,0:T(8,128)(2,1)S(1)}, u32[]{:S(2)}, u32[]{:S(2)}) collective-permute-start(bf16[4,2,128,256]{3,2,1,0:T(8,128)(2,1)} %get-tuple-element.133), channel_id=1, source_target_pairs={{0,12},{4,0},{8,4},{12,8},{1,13},{5,1},{9,5},{13,9},{2,14},{6,2},{... | collective-permute-start | bytes 1572872 | tf_op jit(solution)/shard_map/ppermute | solution.py:16
  34.4 46.2 %collective-permute-start.4 = (bf16[4,2,128,256]{3,2,1,0:T(8,128)(2,1)}, bf16[4,2,128,256]{3,2,1,0:T(8,128)(2,1)}, u32[]{:S(2)}, u32[]{:S(2)}) collective-permute-start(bf16[4,2,128,256]{3,2,1,0:T(8,128)(2,1)} %get-tuple-element.134), channel_id=1, source_target_pairs={{0,8},{4,12},{8,0},{12,4},{1,9},{5,13},{9,1},{13,5},{2,10},{6,14},... | collective-permute-start | bytes 1572872 | tf_op jit(solution)/shard_map/ppermute | solution.py:16
  81.8 0.6 copy-start.9
  82.7 1.2 %copy-start.1 = (f32[2,8,128,128]{3,2,1,0:T(8,128)S(1)}, f32[2,8,128,128]{3,2,1,0:T(8,128)}, u32[]{:S(2)}) copy-start(f32[2,8,128,128]{3,2,1,0:T(8,128)} %convolution_add_fusion) | copy-start | bytes 3145732
